TPU v7x, 32 devices: a whole 2x2x4 slice. The times are simulated.
32 devices in a mesh: blk: 8 (over z, core), vb: 4 (over y, x).
Axes of the slice: x: 2, y: 2, z: 4, core: 2. Of those that a mesh axis runs over, the one named last changes fastest.
Arguments:
- amplitudes: float32 [32, 1024, 1024], P('blk', 'vb'), may hold values from -6 to 6
- integrals: float32 [2048, 1024], P('blk'), may hold values from -0.5 to 0.5
- row_orbitals: int32 [2048], P('blk'), may hold values from 0 to 1023
- pair_orbitals: int32 [32, 2], P('blk'), may hold values from 0 to 255
- occupied_energy: float32 [256], replicated, may hold values from -2 to -0.5
- virtual_energy: float32 [1024], replicated, may hold values from 0.5 to 3
Outputs:
- density: float32 [32, 1024, 1024], P('blk', 'vb')
All inputs are finite; a program needn't handle non-finite values.
Results may differ from a plain program's by a relative error of at most 0.0003.
Values sent between devices are 32-bit elements; how exact they have to be, the bound alone decides.
No kernel may reach another device: no remote copies, remote signals or barrier semaphores. Data moves between devices by JAX's collectives and lax.ppermute only.
A program may use at most 64 MiB of HBM per device.

v0:
```python
import jax
import jax.numpy as jnp
from jax import lax
from jax.sharding import PartitionSpec as P

HOPS = 5
PREC = lax.Precision.HIGH


def roll_lanes(x, shift, axis):
    size = x.shape[axis]
    doubled = jnp.concatenate([x, x], axis=axis)
    return lax.dynamic_slice_in_dim(doubled, (size - shift) % size, size, axis)


def window_blocks(packed):
    nb = lax.axis_size("blk")
    even = range(0, nb, 2)
    core = lax.axis_index("blk") % 2

    def perm(x, pairs):
        return lax.ppermute(x, "blk", [(s % nb, t % nb) for s, t in pairs])

    a = perm(packed, [(d - 2, d) for d in even] + [(d + 3, d + 1) for d in even])
    b = perm(packed, [(d - 1, d) for d in even] + [(d + 2, d + 1) for d in even])
    c = perm(b, [(d + 3, d + 1) for d in even])
    swap = [(d, d + 1) for d in even] + [(d + 1, d) for d in even]
    e = perm(packed, swap)
    f = perm(b, swap)
    g = perm(a, [(d + 1, d) for d in even])
    last = jnp.where(core == 0, g, c)
    return [packed, e, b, a, f, last]


def local(amplitudes, integrals, row_orbitals, pair_orbitals, occupied_energy, virtual_energy):
    assert HOPS == 5 and lax.axis_size("blk") % 2 == 0
    width = virtual_energy.shape[0]
    rows = integrals.shape[0]
    nv = lax.axis_size("vb")
    quarter = width // nv
    q = lax.axis_index("vb")
    qstart = q * quarter
    row_energy = jnp.take(virtual_energy, row_orbitals, axis=0)
    pair_energy = (
        jnp.take(occupied_energy, pair_orbitals[:, 0], axis=0)
        + jnp.take(occupied_energy, pair_orbitals[:, 1], axis=0)
    )
    own_virtual = lax.dynamic_slice_in_dim(virtual_energy, qstart, quarter, 0)

    pieces = [lax.dynamic_slice_in_dim(amplitudes, qstart, quarter, 2)]
    for k in range(1, nv):
        dest_start = ((q + k) % nv) * quarter
        send = lax.dynamic_slice_in_dim(amplitudes, dest_start, quarter, 2)
        pieces.append(lax.ppermute(send, "vb", [(i, (i + k) % nv) for i in range(nv)]))
    rest = jnp.concatenate(pieces[1:], axis=1)

    reversed_cols = jnp.concatenate(
        [integrals[:, ((-k) % nv) * quarter:((-k) % nv + 1) * quarter] for k in range(nv)], axis=1
    )
    rotated = roll_lanes(reversed_cols, qstart, 1)
    erows = -(-rows // width)
    erows_padded = -(-erows // 8) * 8
    energy_rows = jnp.pad(row_energy, (0, erows_padded * width - rows)).reshape(erows_padded, width)
    packed = jnp.concatenate([rotated, energy_rows], axis=0)

    window = [(item[:rows], item[rows:].reshape(-1)[:rows]) for item in window_blocks(packed)]

    def scaled_of(block, energies):
        weighted = jnp.einsum(
            "rb,pba->rpa", block[:, :quarter], pieces[0], precision=PREC, preferred_element_type=jnp.float32
        ) + jnp.einsum(
            "rb,pba->rpa", block[:, quarter:], rest, precision=PREC, preferred_element_type=jnp.float32
        )
        denom = (energies[:, None] + own_virtual[None, :])[:, None, :] - pair_energy[None, :, None]
        return weighted / denom

    def density(cols, blocks):
        total = None
        for block, scaled in blocks:
            part = jnp.einsum(
                "rc,rpa->pca", block[:, cols], scaled, precision=PREC, preferred_element_type=jnp.float32
            )
            total = part if total is None else total + part
        return total

    first = [(block, scaled_of(block, energies)) for block, energies in window[:4]]
    remote_first = density(slice(quarter, None), first)
    own_first = density(slice(0, quarter), first)
    late, remote_first, own_first = lax.optimization_barrier((window[4:], remote_first, own_first))
    last = [(block, scaled_of(block, energies)) for block, energies in late]
    remote = remote_first + density(slice(quarter, None), last)
    received = [None] * nv
    for k in range(1, nv):
        chunk = remote[:, (k - 1) * quarter:k * quarter]
        received[k] = lax.ppermute(chunk, "vb", [(i, (i - k) % nv) for i in range(nv)])
    received[0] = own_first + density(slice(0, quarter), last)
    gathered = jnp.concatenate(received, axis=2)
    return roll_lanes(gathered, qstart, 2)


def solution(mesh):
    return jax.shard_map(
        local,
        mesh=mesh,
        in_specs=(P("blk", "vb", None), P("blk", None), P("blk"), P("blk", None), P(), P()),
        out_specs=P("blk", "vb", None),
        check_vma=False,
    )
```

profile of v0, /device:TPU:0, one launch (start us, length us, event | category | flops | bytes accessed | tf_op | source)
XLA Modules:
  0.0 182.2 jit_solution(7158619710453488946)
XLA Ops:
  0.0 3.8 %constant_dynamic-slice_fusion.1 = (f32[4,256,256]{2,1,0:T(8,128)}, f32[4,256,256]{2,1,0:T(8,128)}, f32[4,256,256]{2,1,0:T(8,128)}) fusion(f32[4,256,1024]{2,1,0:T(8,128)} %param.8, s32[]{:T(128)S(6)} %select_n.81, s32[]{:T(128)S(6)} %select_n.77, s32[]{:T(128)S(6)} %select_n.79), kind=kLoop, calls=%fused_computation.120 | loop fusion | bytes 6291468 | tf_op jit(solution)/shard_map/dynamic_slice | solution.py:53
  3.8 3.9 %collective-permute-start.7 = (f32[4,256,256]{2,1,0:T(8,128)}, f32[4,256,256]{2,1,0:T(8,128)}, u32[]{:S(2)}, u32[]{:S(2)}) collective-permute-start(f32[4,256,256]{2,1,0:T(8,128)} %get-tuple-element.20), channel_id=1, source_target_pairs={{0,3},{1,0},{2,1},{3,2},{4,7},{5,4},{6,5},{7,6},{8,11},{9,8},{10,9... | collective-permute-start | bytes 3145736 | tf_op jit(solution)/shard_map/ppermute | solution.py:54
  7.7 1.1 collective-permute-start.6
  9.1 1.4 gather_fusion
  10.5 0.3 constant_dynamic-slice_fusion.4
  10.9 1.1 pad_maximum_fusion
  12.0 1.6 collective-permute-start.2
  13.6 0.1 dynamic_slice.26
  13.7 0.6 gather_fusion.2
  14.3 0.6 gather_fusion.1
  14.9 1.9 %fusion.26 = f32[256,4,256]{2,0,1:T(8,128)S(1)} fusion(f32[4,256,1024]{2,1,0:T(8,128)} %param.8, s32[]{:T(128)S(6)} %select_n.75, f32[256,2048]{1,0:T(8,128)S(1)} %slice_dynamic-update-slice_fusion.1, s32[]{:T(128)S(6)} %select_n.69), kind=kOutput, calls=%fused_computation.45 | convolution fusion | flops 402653184 | bytes 2359304 | tf_op jit(solution)/shard_map/rb,pba->rpa/dot_general | solution.py:69
  16.8 37.2 %collective-permute-done.5 = f32[4,256,256]{2,1,0:T(8,128)} collective-permute-done((f32[4,256,256]{2,1,0:T(8,128)}, f32[4,256,256]{2,1,0:T(8,128)}, u32[]{:S(2)}, u32[]{:S(2)}) %collective-permute-start.5) | collective-permute-done | bytes 1048608 | tf_op jit(solution)/shard_map/ppermute | solution.py:54
  54.0 2.1 %collective-permute-start = (f32[264,1024]{1,0:T(8,128)}, f32[264,1024]{1,0:T(8,128)S(1)}, u32[]{:S(2)}, u32[]{:S(2)}) collective-permute-start(f32[264,1024]{1,0:T(8,128)} %pad_maximum_fusion), channel_id=1, source_target_pairs={{28,0},{4,8},{12,16},{20,24},{8,4},{16,12},{24,20},{0,28},{29,1},{... | collective-permute-start | bytes 3244040 | tf_op jit(solution)/shard_map/ppermute | solution.py:22
  56.2 1.3 constant_dynamic-update-slice_fusion.2
  57.5 1.3 constant_dynamic-update-slice_fusion.1
  58.8 1.3 constant_dynamic-update-slice_fusion
  60.1 0.8 slice_bitcast_fusion.22
  60.9 20.9 %collective-permute-done = f32[264,1024]{1,0:T(8,128)S(1)} collective-permute-done((f32[264,1024]{1,0:T(8,128)}, f32[264,1024]{1,0:T(8,128)S(1)}, u32[]{:S(2)}, u32[]{:S(2)}) %collective-permute-start) | collective-permute-done | bytes 1081376 | tf_op jit(solution)/shard_map/ppermute | solution.py:22
  81.9 0.2 broadcast_add_fusion.2
  82.1 1.8 %fusion.2 = f32[256,4,256]{2,0,1:T(8,128)S(1)} fusion(f32[256,4,256]{2,0,1:T(8,128)S(1)} %fusion.26, f32[4,768,256]{2,1,0:T(8,128)S(1)} %constant_dynamic-update-slice_fusion, f32[256,2048]{1,0:T(8,128)S(1)} %slice_dynamic-update-slice_fusion.1, s32[]{:T(128)S(6)} %add.267, f32[4]{0:T(128)S(1)} %fusion.55, f32[256,256]{1,0:T(8,128)S(1)} %get-tuple-element.31), kind=kOutput, calls=%fused_computation.10 | convolution fusion | flops 1208745984 | bytes 6291972 | tf_op jit(solution)/shard_map/rb,pba->rpa/dot_general | solution.py:71
  83.9 1.1 fusion.45
  85.0 1.3 collective-permute-start.3
  86.3 0.9 collective-permute-start.4
  87.2 4.3 %collective-permute-start.1 = (f32[264,1024]{1,0:T(8,128)S(1)}, f32[264,1024]{1,0:T(8,128)S(1)}, u32[]{:S(2)}, u32[]{:S(2)}) collective-permute-start(f32[264,1024]{1,0:T(8,128)S(1)} %collective-permute-done), channel_id=1, source_target_pairs={{0,4},{8,12},{16,20},{24,28},{4,0},{12,8},{20,16},{28,24},{1,5},{9... | collective-permute-start | bytes 3244040 | tf_op jit(solution)/shard_map/ppermute | solution.py:22
  91.6 1.7 fusion.33
  93.3 1.7 fusion.31
  95.1 3.0 %fusion.29 = f32[256,4,256]{2,0,1:T(8,128)S(1)} fusion(f32[4,768,256]{2,1,0:T(8,128)S(1)} %constant_dynamic-update-slice_fusion, f32[264,1024]{1,0:T(8,128)} %collective-permute-done.8), kind=kOutput, calls=%fused_computation.48 | convolution fusion | flops 1207959552 | bytes 4980736 | tf_op jit(solution)/shard_map/rb,pba->rpa/dot_general | solution.py:71
  98.1 0.8 fusion.6
  98.9 1.0 fusion.44
  100.0 0.8 fusion.7
  100.8 1.7 fusion.30
  102.5 1.8 fusion.8
  104.3 2.0 %convolution_add_fusion.5 = f32[4,256,256]{2,1,0:T(8,128)S(1)} fusion(f32[4,256,256]{2,1,0:T(8,128)S(1)} %fusion.45, f32[256,4,256]{2,0,1:T(8,128)S(1)} %fusion.8, f32[264,1024]{1,0:T(8,128)} %collective-permute-done.8), kind=kOutput, calls=%fused_computation.16 | convolution fusion | flops 402915328 | bytes 3407872 | tf_op jit(solution)/shard_map/rc,rpa->pca/dot_general | solution.py:80
  106.3 1.1 fusion.5
  107.3 2.1 %fusion.34 = f32[4,256,768]{2,1,0:T(8,128)S(1)} fusion(f32[256,4,256]{2,0,1:T(8,128)S(1)} %fusion.2, f32[256,2048]{1,0:T(8,128)S(1)} %slice_dynamic-update-slice_fusion.1, s32[]{:T(128)S(6)} %add.267), kind=kOutput, calls=%fused_computation.53 | convolution fusion | flops 1207959552 | bytes 4980740 | tf_op jit(solution)/shard_map/rc,rpa->pca/dot_general | solution.py:80
  109.4 2.8 %fusion.28 = f32[4,256,768]{2,1,0:T(8,128)S(1)} fusion(f32[256,4,256]{2,0,1:T(8,128)S(1)} %fusion.8, f32[264,1024]{1,0:T(8,128)} %collective-permute-done.8), kind=kOutput, calls=%fused_computation.47 | convolution fusion | flops 1207959552 | bytes 4980736 | tf_op jit(solution)/shard_map/rc,rpa->pca/dot_general | solution.py:80
  112.3 2.5 %add_bitcast_fusion = f32[4,768,256]{1,2,0:T(8,128)S(1)} fusion(f32[4,256,768]{2,1,0:T(8,128)S(1)} %fusion.30, f32[4,256,768]{2,1,0:T(8,128)S(1)} %fusion.34, f32[4,256,768]{2,1,0:T(8,128)S(1)} %fusion.28, f32[256,4,256]{2,0,1:T(8,128)S(1)} %fusion.6, f32[264,1024]{1,0:T(8,128)S(1)} %collective-permute-done.2), kind=kOutput, calls=%fused_computation.4 | convolution fusion | flops 1210318848 | bytes 14417920 | tf_op jit(solution)/shard_map/rc,rpa->pca/dot_general | solution.py:80
  114.8 0.2 broadcast_select_fusion
  114.9 0.1 slice.163
  115.1 0.1 slice.160
  115.2 0.7 fusion.21
  115.9 0.7 fusion.19
  116.6 0.1 broadcast_add_fusion
  116.7 1.8 fusion
  118.5 1.7 fusion.9
  120.2 1.8 fusion.1
  122.1 1.7 fusion.12
  123.8 0.8 bitcast_add_fusion
  124.6 0.3 fusion.56
  125.0 1.5 collective-permute-start.9
  126.4 0.6 collective-permute-start.11
  127.0 0.9 collective-permute-start.10
  127.9 1.0 fusion.37
  129.0 1.0 fusion.3
  130.0 0.2 constant_dynamic-update-slice_fusion.10
  130.2 20.8 %collective-permute-done.9 = f32[4,256,256]{1,2,0:T(8,128)S(1)} collective-permute-done((f32[4,256,256]{1,2,0:T(8,128)S(1)}, f32[4,256,256]{1,2,0:T(8,128)S(1)}, u32[]{:S(2)}, u32[]{:S(2)}) %collective-permute-start.9) | collective-permute-done | bytes 1048608 | tf_op jit(solution)/shard_map/ppermute | solution.py:95
  151.1 22.9 %collective-permute-done.10 = f32[4,256,256]{1,2,0:T(8,128)S(1)} collective-permute-done((f32[4,256,256]{1,2,0:T(8,128)S(1)}, f32[4,256,256]{1,2,0:T(8,128)S(1)}, u32[]{:S(2)}, u32[]{:S(2)}) %collective-permute-start.10) | collective-permute-done | bytes 1048608 | tf_op jit(solution)/shard_map/ppermute | solution.py:95
  174.1 0.1 constant_dynamic-update-slice_fusion.7
  174.2 0.1 constant_dynamic-update-slice_fusion.6
  174.3 0.1 constant_dynamic-update-slice_fusion.5
  174.4 0.1 constant_dynamic-update-slice_fusion.4
  174.4 0.1 constant_dynamic-update-slice_fusion.3
  174.5 2.4 %constant_dynamic-slice_fusion = f32[4,256,1024]{1,2,0:T(8,128)} fusion(f32[4,256,2048]{1,2,0:T(8,128)S(1)} %constant_dynamic-update-slice_fusion.3, s32[]{:T(128)S(6)} %select_n.69), kind=kLoop, calls=%fused_computation.119 | loop fusion | bytes 8388612 | tf_op jit(solution)/shard_map/dynamic_slice | solution.py:13
  176.9 5.3 %copy.32 = f32[4,256,1024]{2,1,0:T(8,128)} copy(f32[4,256,1024]{1,2,0:T(8,128)} %constant_dynamic-slice_fusion) | data formatting | bytes 8388608 | tf_op jit(solution)/shard_map/dynamic_slice | solution.py:13
  (56 shorter events, 0.5 us)
Async XLA Ops:
  0.0 13.7 %copy-start = (f32[256]{0:T(256)S(1)}, f32[256]{0:T(256)}, u32[]{:S(2)}) copy-start(f32[256]{0:T(256)} %param.12) | copy-start | bytes 3076
  0.0 8.8 %copy-start.5 = (s32[256]{0:T(256)S(1)}, s32[256]{0:T(256)}, u32[]{:S(2)}) copy-start(s32[256]{0:T(256)} %param.10) | copy-start | bytes 3076
  0.0 8.8 %copy-start.4 = (f32[256,1024]{1,0:T(8,128)S(1)}, f32[256,1024]{1,0:T(8,128)}, u32[]{:S(2)}) copy-start(f32[256,1024]{1,0:T(8,128)} %param.9) | copy-start | bytes 3145732
  3.8 5.3 %copy-start.2 = (f32[1024]{0:T(1024)S(1)}, f32[1024]{0:T(1024)}, u32[]{:S(2)}) copy-start(f32[1024]{0:T(1024)} %param.13) | copy-start | bytes 12292
  3.8 55.0 %collective-permute-start.7 = (f32[4,256,256]{2,1,0:T(8,128)}, f32[4,256,256]{2,1,0:T(8,128)}, u32[]{:S(2)}, u32[]{:S(2)}) collective-permute-start(f32[4,256,256]{2,1,0:T(8,128)} %get-tuple-element.20), channel_id=1, source_target_pairs={{0,3},{1,0},{2,1},{3,2},{4,7},{5,4},{6,5},{7,6},{8,11},{9,8},{10,9... | collective-permute-start | bytes 3145736 | tf_op jit(solution)/shard_map/ppermute | solution.py:54
  7.7 46.3 %collective-permute-start.5 = (f32[4,256,256]{2,1,0:T(8,128)}, f32[4,256,256]{2,1,0:T(8,128)}, u32[]{:S(2)}, u32[]{:S(2)}) collective-permute-start(f32[4,256,256]{2,1,0:T(8,128)} %get-tuple-element.21), channel_id=1, source_target_pairs={{0,1},{1,2},{2,3},{3,0},{4,5},{5,6},{6,7},{7,4},{8,9},{9,10},{10,1... | collective-permute-start | bytes 3145736 | tf_op jit(solution)/shard_map/ppermute | solution.py:54
  7.7 49.7 %collective-permute-start.6 = (f32[4,256,256]{2,1,0:T(8,128)}, f32[4,256,256]{2,1,0:T(8,128)}, u32[]{:S(2)}, u32[]{:S(2)}) collective-permute-start(f32[4,256,256]{2,1,0:T(8,128)} %get-tuple-element.22), channel_id=1, source_target_pairs={{0,2},{1,3},{2,0},{3,1},{4,6},{5,7},{6,4},{7,5},{8,10},{9,11},{10,... | collective-permute-start | bytes 3145736 | tf_op jit(solution)/shard_map/ppermute | solution.py:54
  9.0 4.6 %copy-start.6 = (s32[4,2]{0,1:T(2,128)S(1)}, s32[4,2]{0,1:T(2,128)}, u32[]{:S(2)}) copy-start(s32[4,2]{0,1:T(2,128)} %param.11) | copy-start | bytes 100
  12.0 48.1 %collective-permute-start.8 = (f32[264,1024]{1,0:T(8,128)}, f32[264,1024]{1,0:T(8,128)}, u32[]{:S(2)}, u32[]{:S(2)}) collective-permute-start(f32[264,1024]{1,0:T(8,128)} %pad_maximum_fusion), channel_id=1, source_target_pairs={{0,4},{8,12},{16,20},{24,28},{4,0},{12,8},{20,16},{28,24},{1,5},{9... | collective-permute-start | bytes 3244040 | tf_op jit(solution)/shard_map/ppermute | solution.py:22
  12.0 48.9 %collective-permute-start.2 = (f32[264,1024]{1,0:T(8,128)}, f32[264,1024]{1,0:T(8,128)S(1)}, u32[]{:S(2)}, u32[]{:S(2)}) collective-permute-start(f32[264,1024]{1,0:T(8,128)} %pad_maximum_fusion), channel_id=1, source_target_pairs={{24,0},{0,8},{8,16},{16,24},{12,4},{20,12},{28,20},{4,28},{25,1},{... | collective-permute-start | bytes 3244040 | tf_op jit(solution)/shard_map/ppermute | solution.py:22
  54.0 27.8 %collective-permute-start = (f32[264,1024]{1,0:T(8,128)}, f32[264,1024]{1,0:T(8,128)S(1)}, u32[]{:S(2)}, u32[]{:S(2)}) collective-permute-start(f32[264,1024]{1,0:T(8,128)} %pad_maximum_fusion), channel_id=1, source_target_pairs={{28,0},{4,8},{12,16},{20,24},{8,4},{16,12},{24,20},{0,28},{29,1},{... | collective-permute-start | bytes 3244040 | tf_op jit(solution)/shard_map/ppermute | solution.py:22
  85.0 29.7 %collective-permute-start.3 = (f32[264,1024]{1,0:T(8,128)S(1)}, f32[264,1024]{1,0:T(8,128)S(1)}, u32[]{:S(2)}, u32[]{:S(2)}) collective-permute-start(f32[264,1024]{1,0:T(8,128)S(1)} %collective-permute-done.2), channel_id=1, source_target_pairs={{4,0},{12,8},{20,16},{28,24},{5,1},{13,9},{21,17},{29,25},{6,2},{1... | collective-permute-start | bytes 3244040 | tf_op jit(solution)/shard_map/ppermute | solution.py:22
  86.3 28.4 %collective-permute-start.4 = (f32[264,1024]{1,0:T(8,128)S(1)}, f32[264,1024]{1,0:T(8,128)S(1)}, u32[]{:S(2)}, u32[]{:S(2)}) collective-permute-start(f32[264,1024]{1,0:T(8,128)S(1)} %collective-permute-done), channel_id=1, source_target_pairs={{12,4},{20,12},{28,20},{4,28},{13,5},{21,13},{29,21},{5,29},{14,6}... | collective-permute-start | bytes 3244040 | tf_op jit(solution)/shard_map/ppermute | solution.py:22
  87.2 27.8 %collective-permute-start.1 = (f32[264,1024]{1,0:T(8,128)S(1)}, f32[264,1024]{1,0:T(8,128)S(1)}, u32[]{:S(2)}, u32[]{:S(2)}) collective-permute-start(f32[264,1024]{1,0:T(8,128)S(1)} %collective-permute-done), channel_id=1, source_target_pairs={{0,4},{8,12},{16,20},{24,28},{4,0},{12,8},{20,16},{28,24},{1,5},{9... | collective-permute-start | bytes 3244040 | tf_op jit(solution)/shard_map/ppermute | solution.py:22
  95.1 3.1 %copy-start.3 = (f32[4,256,1024]{2,1,0:T(8,128)S(1)}, f32[4,256,1024]{2,1,0:T(8,128)}, u32[]{:S(2)}) copy-start(f32[4,256,1024]{2,1,0:T(8,128)} %param.8) | copy-start | bytes 12582916
  125.0 26.1 %collective-permute-start.9 = (f32[4,256,256]{1,2,0:T(8,128)S(1)}, f32[4,256,256]{1,2,0:T(8,128)S(1)}, u32[]{:S(2)}, u32[]{:S(2)}) collective-permute-start(f32[4,256,256]{1,2,0:T(8,128)S(1)} %get-tuple-element.25), channel_id=1, source_target_pairs={{0,3},{1,0},{2,1},{3,2},{4,7},{5,4},{6,5},{7,6},{8,11},{9,8},{10,9... | collective-permute-start | bytes 3145736 | tf_op jit(solution)/shard_map/ppermute | solution.py:95
  126.4 47.7 %collective-permute-start.11 = (f32[4,256,256]{1,2,0:T(8,128)S(1)}, f32[4,256,256]{1,2,0:T(8,128)S(1)}, u32[]{:S(2)}, u32[]{:S(2)}) collective-permute-start(f32[4,256,256]{1,2,0:T(8,128)S(1)} %get-tuple-element.23), channel_id=1, source_target_pairs={{0,1},{1,2},{2,3},{3,0},{4,5},{5,6},{6,7},{7,4},{8,9},{9,10},{10,1... | collective-permute-start | bytes 3145736 | tf_op jit(solution)/shard_map/ppermute | solution.py:95
  127.0 47.0 %collective-permute-start.10 = (f32[4,256,256]{1,2,0:T(8,128)S(1)}, f32[4,256,256]{1,2,0:T(8,128)S(1)}, u32[]{:S(2)}, u32[]{:S(2)}) collective-permute-start(f32[4,256,256]{1,2,0:T(8,128)S(1)} %get-tuple-element.24), channel_id=1, source_target_pairs={{0,2},{1,3},{2,0},{3,1},{4,6},{5,7},{6,4},{7,5},{8,10},{9,11},{10,... | collective-permute-start | bytes 3145736 | tf_op jit(solution)/shard_map/ppermute | solution.py:95
  174.5 7.7 %copy-start.1 = (f32[256]{0:T(256)S(1)}, f32[256]{0:T(256)}, u32[]{:S(2)}) copy-start(f32[256]{0:T(256)} %param.12) | copy-start | bytes 3076
where the time goes:
time: 183 us; the launch traced here: 182 us
  waiting for transfers between devices  102 us (56%)
  matrix products  38.3 us (21%)
  local copies, waits for them, and re-layouts  20.5 us (11%)
  starting transfers between devices  18.2 us (10%)
  other arithmetic  2.69 us (1%)
    ppermute x3, waiting for transfers between devices, local(): lax.ppermute(chunk, 'vb', [(i, (i - k) % nv) for i in range(nv)])  43.7 us
    ppermute x3, waiting for transfers between devices, local(): lax.ppermute(send, 'vb', [(i, (i + k) % nv) for i in range(nv)])  37.2 us
    ppermute x6, waiting for transfers between devices, perm(): return lax.ppermute(x, 'blk', [(s % nb, t % nb) for s, t in pairs])  20.9 us
    dot_general x12, matrix products, density(): jnp.einsum('rc,rpa->pca', block[:, cols], scaled, precision=PREC, preferr...  19.7 us
    dot_general x6, matrix products, scaled_of(): jnp.einsum('rb,pba->rpa', block[:, quarter:], rest, precision=PREC, prefe...  12 us
    ppermute x6, starting transfers between devices, perm(): return lax.ppermute(x, 'blk', [(s % nb, t % nb) for s, t in pairs])  10.2 us
    dynamic_slice x3, local copies, waits for them, and re-layouts, roll_lanes(): return lax.dynamic_slice_in_dim(doubled, (size - shift) % size, size, axis)  8.04 us
    dot_general x6, matrix products, scaled_of(): jnp.einsum('rb,pba->rpa', block[:, :quarter], pieces[0], precision=PREC,...  6.63 us
  transfers between devices with their start and end apart: 12, of which 4 were waited for; matrix products, arithmetic and copies ran while one was open for 20% of the time, Pallas kernels for 0%

commit v1 on v0

--- a/solution.py
+++ b/solution.py
@@ -83,10 +83,12 @@
             total = part if total is None else total + part
         return total
 
-    first = [(block, scaled_of(block, energies)) for block, energies in window[:4]]
+    early_blocks = [window[0], window[2], window[3]]
+    late_blocks = [window[1], window[4], window[5]]
+    first = [(block, scaled_of(block, energies)) for block, energies in early_blocks]
     remote_first = density(slice(quarter, None), first)
     own_first = density(slice(0, quarter), first)
-    late, remote_first, own_first = lax.optimization_barrier((window[4:], remote_first, own_first))
+    late, remote_first, own_first = lax.optimization_barrier((late_blocks, remote_first, own_first))
     last = [(block, scaled_of(block, energies)) for block, energies in late]
     remote = remote_first + density(slice(quarter, None), last)
     received = [None] * nv

time: 183 us -> 170 us (0.929)
  waiting for transfers between devices: 102 us -> 83.6 us
  matrix products: 38.3 us -> 41.8 us
  starting transfers between devices: 18.2 us -> 20.8 us
    ppermute x6, waiting for transfers between devices: 20.9 us -> 3.73 us  [perm(): return lax.ppermute(x, 'blk', [(s % nb, t % nb) for s, t in pairs])]
  transfers between devices with their start and end apart: 12 -> 12, of which waited for: 4 -> 4; matrix products, arithmetic and copies ran while one was open for 20% -> 23% of each run, Pallas kernels for 0% -> 0%
where the time goes in v1:
time: 170 us; the launch traced here: 169 us
  waiting for transfers between devices  83.6 us (49%)
  matrix products  41.8 us (25%)
  starting transfers between devices  20.8 us (12%)
  local copies, waits for them, and re-layouts  20.1 us (12%)
  other arithmetic  2.63 us (2%)
    ppermute x3, waiting for transfers between devices, local(): lax.ppermute(chunk, 'vb', [(i, (i - k) % nv) for i in range(nv)])  43.4 us
    ppermute x3, waiting for transfers between devices, local(): lax.ppermute(send, 'vb', [(i, (i + k) % nv) for i in range(nv)])  36.4 us
    dot_general x12, matrix products, density(): jnp.einsum('rc,rpa->pca', block[:, cols], scaled, precision=PREC, preferr...  21.1 us
    dot_general x6, matrix products, scaled_of(): jnp.einsum('rb,pba->rpa', block[:, quarter:], rest, precision=PREC, prefe...  13 us
    ppermute x6, starting transfers between devices, perm(): return lax.ppermute(x, 'blk', [(s % nb, t % nb) for s, t in pairs])  11.7 us
    dynamic_slice x3, local copies, waits for them, and re-layouts, roll_lanes(): return lax.dynamic_slice_in_dim(doubled, (size - shift) % size, size, axis)  8.04 us
    dot_general x6, matrix products, scaled_of(): jnp.einsum('rb,pba->rpa', block[:, :quarter], pieces[0], precision=PREC,...  7.66 us
    ppermute x3, starting transfers between devices, local(): lax.ppermute(send, 'vb', [(i, (i + k) % nv) for i in range(nv)])  5.03 us
  transfers between devices with their start and end apart: 12, of which 4 were waited for; matrix products, arithmetic and copies ran while one was open for 23% of the time, Pallas kernels for 0%

profile of v1, /device:TPU:0, one launch (start us, length us, event | category | flops | bytes accessed | tf_op | source)
XLA Modules:
  0.0 169.5 jit_solution(7881143187496137260)
XLA Ops:
  0.0 3.7 %constant_dynamic-slice_fusion.1 = (f32[4,256,256]{2,1,0:T(8,128)}, f32[4,256,256]{2,1,0:T(8,128)}, f32[4,256,256]{2,1,0:T(8,128)}) fusion(f32[4,256,1024]{2,1,0:T(8,128)} %param.8, s32[]{:T(128)S(6)} %select_n.81, s32[]{:T(128)S(6)} %select_n.77, s32[]{:T(128)S(6)} %select_n.79), kind=kLoop, calls=%fused_computation.124 | loop fusion | bytes 6291468 | tf_op jit(solution)/shard_map/dynamic_slice | solution.py:53
  3.7 3.9 %collective-permute-start.8 = (f32[4,256,256]{2,1,0:T(8,128)}, f32[4,256,256]{2,1,0:T(8,128)S(1)}, u32[]{:S(2)}, u32[]{:S(2)}) collective-permute-start(f32[4,256,256]{2,1,0:T(8,128)} %get-tuple-element.24), channel_id=1, source_target_pairs={{0,3},{1,0},{2,1},{3,2},{4,7},{5,4},{6,5},{7,6},{8,11},{9,8},{10,9... | collective-permute-start | bytes 3145736 | tf_op jit(solution)/shard_map/ppermute | solution.py:54
  7.7 1.1 collective-permute-start.7
  9.0 1.4 gather_fusion
  10.5 0.3 constant_dynamic-slice_fusion.4
  10.8 1.1 pad_maximum_fusion
  11.9 1.6 collective-permute-start.3
  13.5 0.8 collective-permute-start.1
  14.3 0.1 dynamic_slice.26
  14.4 0.6 gather_fusion.2
  15.0 0.6 gather_fusion.1
  15.7 1.9 %fusion.31 = f32[256,4,256]{2,0,1:T(8,128)S(1)} fusion(f32[4,256,1024]{2,1,0:T(8,128)} %param.8, s32[]{:T(128)S(6)} %select_n.75, f32[256,2048]{1,0:T(8,128)S(1)} %slice_dynamic-update-slice_fusion.1, s32[]{:T(128)S(6)} %select_n.69), kind=kOutput, calls=%fused_computation.50 | convolution fusion | flops 402653184 | bytes 2359304 | tf_op jit(solution)/shard_map/rb,pba->rpa/dot_general | solution.py:69
  17.6 36.4 %collective-permute-done.6 = f32[4,256,256]{2,1,0:T(8,128)} collective-permute-done((f32[4,256,256]{2,1,0:T(8,128)}, f32[4,256,256]{2,1,0:T(8,128)}, u32[]{:S(2)}, u32[]{:S(2)}) %collective-permute-start.6) | collective-permute-done | bytes 1048608 | tf_op jit(solution)/shard_map/ppermute | solution.py:54
  54.0 1.3 constant_dynamic-update-slice_fusion.2
  55.3 1.3 constant_dynamic-update-slice_fusion.1
  56.6 0.1 constant_dynamic-update-slice_fusion
  56.7 0.8 slice_bitcast_fusion.12
  57.5 3.7 %collective-permute-done.1 = f32[264,1024]{1,0:T(8,128)} collective-permute-done((f32[264,1024]{1,0:T(8,128)}, f32[264,1024]{1,0:T(8,128)}, u32[]{:S(2)}, u32[]{:S(2)}) %collective-permute-start.1) | collective-permute-done | bytes 1081376 | tf_op jit(solution)/shard_map/ppermute | solution.py:22
  61.2 0.8 slice_bitcast_fusion.13
  62.0 0.2 broadcast_add_fusion.3
  62.1 1.9 %fusion.3 = f32[256,4,256]{2,0,1:T(8,128)S(1)} fusion(f32[256,4,256]{2,0,1:T(8,128)S(1)} %fusion.31, f32[4,768,256]{2,1,0:T(8,128)S(1)} %constant_dynamic-update-slice_fusion, f32[256,2048]{1,0:T(8,128)S(1)} %slice_dynamic-update-slice_fusion.1, s32[]{:T(128)S(6)} %add.267, f32[4]{0:T(128)S(1)} %fusion.60, f32[256,256]{1,0:T(8,128)S(1)} %get-tuple-element.35), kind=kOutput, calls=%fused_computation.12 | convolution fusion | flops 1208745984 | bytes 6291972 | tf_op jit(solution)/shard_map/rb,pba->rpa/dot_general | solution.py:71
  64.0 1.1 fusion.50
  65.1 1.3 collective-permute-start.4
  66.4 0.9 collective-permute-start.5
  67.3 7.1 %collective-permute-start.2 = (f32[264,1024]{1,0:T(8,128)}, f32[264,1024]{1,0:T(8,128)S(1)}, u32[]{:S(2)}, u32[]{:S(2)}) collective-permute-start(f32[264,1024]{1,0:T(8,128)} %collective-permute-done.1), channel_id=1, source_target_pairs={{0,4},{8,12},{16,20},{24,28},{4,0},{12,8},{20,16},{28,24},{1,5},{9... | collective-permute-start | bytes 3244040 | tf_op jit(solution)/shard_map/ppermute | solution.py:22
  74.4 2.8 %fusion.35 = f32[256,4,256]{2,0,1:T(8,128)S(1)} fusion(f32[4,768,256]{2,1,0:T(8,128)S(1)} %constant_dynamic-update-slice_fusion, f32[264,1024]{1,0:T(8,128)} %collective-permute-done.3), kind=kOutput, calls=%fused_computation.54 | convolution fusion | flops 1207959552 | bytes 4980736 | tf_op jit(solution)/shard_map/rb,pba->rpa/dot_general | solution.py:71
  77.3 3.0 %fusion.34 = f32[256,4,256]{2,0,1:T(8,128)S(1)} fusion(f32[4,768,256]{2,1,0:T(8,128)S(1)} %constant_dynamic-update-slice_fusion, f32[264,1024]{1,0:T(8,128)} %collective-permute-done.1), kind=kOutput, calls=%fused_computation.53 | convolution fusion | flops 1207959552 | bytes 4980736 | tf_op jit(solution)/shard_map/rb,pba->rpa/dot_general | solution.py:71
  80.3 1.7 %fusion.7 = f32[256,4,256]{2,0,1:T(8,128)S(1)} fusion(f32[256,4,256]{2,0,1:T(8,128)S(1)} %fusion.34, f32[4,256,1024]{2,1,0:T(8,128)S(1)} %copy-done.3, s32[]{:T(128)S(6)} %select_n.75, f32[256,256]{1,0:T(8,128)S(1)} %get-tuple-element.34, f32[4]{0:T(128)S(1)} %fusion.60, f32[264,1024]{1,0:T(8,128)} %collective-permute-done.1), kind=kOutput, calls=%fused_computation.22 | convolution fusion | flops 403439616 | bytes 3670532 | tf_op jit(solution)/shard_map/rb,pba->rpa/dot_general | solution.py:69
  82.0 2.0 %convolution_add_fusion.7 = f32[4,256,256]{2,1,0:T(8,128)S(1)} fusion(f32[4,256,256]{2,1,0:T(8,128)S(1)} %fusion.50, f32[256,4,256]{2,0,1:T(8,128)S(1)} %fusion.7, f32[264,1024]{1,0:T(8,128)} %collective-permute-done.1), kind=kOutput, calls=%fused_computation.18 | convolution fusion | flops 402915328 | bytes 3407872 | tf_op jit(solution)/shard_map/rc,rpa->pca/dot_general | solution.py:80
  84.0 1.8 %fusion.6 = f32[256,4,256]{2,0,1:T(8,128)S(1)} fusion(f32[256,4,256]{2,0,1:T(8,128)S(1)} %fusion.35, f32[4,256,1024]{2,1,0:T(8,128)S(1)} %copy-done.3, s32[]{:T(128)S(6)} %select_n.75, f32[256,256]{1,0:T(8,128)S(1)} %get-tuple-element.33, f32[4]{0:T(128)S(1)} %fusion.60, f32[264,1024]{1,0:T(8,128)} %collective-permute-done.3), kind=kOutput, calls=%fused_computation.20 | convolution fusion | flops 403439616 | bytes 3670532 | tf_op jit(solution)/shard_map/rb,pba->rpa/dot_general | solution.py:69
  85.8 2.0 %fusion.5 = f32[4,256,256]{1,2,0:T(8,128)S(1)} fusion(f32[4,256,256]{2,1,0:T(8,128)S(1)} %convolution_add_fusion.7, f32[256,4,256]{2,0,1:T(8,128)S(1)} %fusion.6, f32[264,1024]{1,0:T(8,128)} %collective-permute-done.3), kind=kOutput, calls=%fused_computation.17 | convolution fusion | flops 402915328 | bytes 3407872 | tf_op jit(solution)/shard_map/rc,rpa->pca/dot_general | solution.py:80
  87.8 1.9 %fusion.36 = f32[4,256,768]{2,1,0:T(8,128)S(1)} fusion(f32[256,4,256]{2,0,1:T(8,128)S(1)} %fusion.3, f32[256,2048]{1,0:T(8,128)S(1)} %slice_dynamic-update-slice_fusion.1, s32[]{:T(128)S(6)} %add.267), kind=kOutput, calls=%fused_computation.55 | convolution fusion | flops 1207959552 | bytes 4980740 | tf_op jit(solution)/shard_map/rc,rpa->pca/dot_general | solution.py:80
  89.7 2.9 %fusion.33 = f32[4,256,768]{2,1,0:T(8,128)S(1)} fusion(f32[256,4,256]{2,0,1:T(8,128)S(1)} %fusion.7, f32[264,1024]{1,0:T(8,128)} %collective-permute-done.1), kind=kOutput, calls=%fused_computation.52 | convolution fusion | flops 1207959552 | bytes 4980736 | tf_op jit(solution)/shard_map/rc,rpa->pca/dot_general | solution.py:80
  92.6 0.1 slice.161
  92.7 3.1 %add_bitcast_fusion = f32[4,768,256]{1,2,0:T(8,128)S(1)} fusion(f32[4,256,768]{2,1,0:T(8,128)S(1)} %fusion.36, f32[4,256,768]{2,1,0:T(8,128)S(1)} %fusion.33, f32[256,4,256]{2,0,1:T(8,128)S(1)} %fusion.6, f32[264,1024]{1,0:T(8,128)} %collective-permute-done.3), kind=kOutput, calls=%fused_computation.4 | convolution fusion | flops 1209532416 | bytes 11272192 | tf_op jit(solution)/shard_map/rc,rpa->pca/dot_general | solution.py:80
  95.9 0.2 broadcast_select_fusion
  96.1 0.1 slice.167
  96.3 0.1 slice.164
  96.4 0.9 fusion.27
  97.3 0.2 broadcast_add_fusion
  97.5 1.8 %fusion.2 = f32[256,4,256]{2,0,1:T(8,128)S(1)} fusion(f32[256,4,256]{2,0,1:T(8,128)S(1)} %fusion.27, f32[4,768,256]{2,1,0:T(8,128)S(1)} %constant_dynamic-update-slice_fusion, f32[256,1024]{1,0:T(8,128)S(1)} %slice.161, f32[256,256]{1,0:T(8,128)S(1)} %get-tuple-element.31, f32[4]{0:T(128)S(1)} %fusion.60), kind=kOutput, calls=%fused_computation.10 | convolution fusion | flops 1208745984 | bytes 6291968 | tf_op jit(solution)/shard_map/rb,pba->rpa/dot_general | solution.py:71
  99.2 1.7 %fusion.14 = f32[4,256,768]{2,1,0:T(8,128)S(1)} fusion(f32[256,4,256]{2,0,1:T(8,128)S(1)} %fusion.2, f32[256,1024]{1,0:T(8,128)S(1)} %slice.161), kind=kOutput, calls=%fused_computation.33 | convolution fusion | flops 1207959552 | bytes 4980736 | tf_op jit(solution)/shard_map/rc,rpa->pca/dot_general | solution.py:80
  101.0 0.7 fusion.25
  101.6 0.7 fusion.23
  102.3 1.8 %fusion = f32[256,4,256]{2,0,1:T(8,128)S(1)} fusion(f32[256,4,256]{2,0,1:T(8,128)S(1)} %fusion.23, f32[4,768,256]{2,1,0:T(8,128)S(1)} %constant_dynamic-update-slice_fusion, f32[256,1024]{1,0:T(8,128)S(1)} %slice.167, f32[256,256]{1,0:T(8,128)S(1)} %get-tuple-element.30, f32[4]{0:T(128)S(1)} %fusion.60), kind=kOutput, calls=%fused_computation.6 | convolution fusion | flops 1208745984 | bytes 6291968 | tf_op jit(solution)/shard_map/rb,pba->rpa/dot_general | solution.py:71
  104.1 1.7 %fusion.8 = f32[4,256,768]{2,1,0:T(8,128)S(1)} fusion(f32[256,4,256]{2,0,1:T(8,128)S(1)} %fusion, f32[256,1024]{1,0:T(8,128)S(1)} %slice.167), kind=kOutput, calls=%fused_computation.27 | convolution fusion | flops 1207959552 | bytes 4980736 | tf_op jit(solution)/shard_map/rc,rpa->pca/dot_general | solution.py:80
  105.8 1.8 %fusion.1 = f32[256,4,256]{2,0,1:T(8,128)S(1)} fusion(f32[256,4,256]{2,0,1:T(8,128)S(1)} %fusion.25, f32[4,768,256]{2,1,0:T(8,128)S(1)} %constant_dynamic-update-slice_fusion, f32[256,1024]{1,0:T(8,128)S(1)} %slice.164, f32[256,256]{1,0:T(8,128)S(1)} %get-tuple-element.32, f32[4]{0:T(128)S(1)} %fusion.60), kind=kOutput, calls=%fused_computation.8 | convolution fusion | flops 1208745984 | bytes 6291968 | tf_op jit(solution)/shard_map/rb,pba->rpa/dot_general | solution.py:71
  107.6 1.7 %fusion.11 = f32[4,256,768]{2,1,0:T(8,128)S(1)} fusion(f32[256,4,256]{2,0,1:T(8,128)S(1)} %fusion.1, f32[256,1024]{1,0:T(8,128)S(1)} %slice.164), kind=kOutput, calls=%fused_computation.30 | convolution fusion | flops 1207959552 | bytes 4980736 | tf_op jit(solution)/shard_map/rc,rpa->pca/dot_general | solution.py:80
  109.3 0.8 bitcast_add_fusion
  110.1 0.3 fusion.61
  110.4 2.4 %collective-permute-start.9 = (f32[4,256,256]{1,2,0:T(8,128)S(1)}, f32[4,256,256]{1,2,0:T(8,128)S(1)}, u32[]{:S(2)}, u32[]{:S(2)}) collective-permute-start(f32[4,256,256]{1,2,0:T(8,128)S(1)} %get-tuple-element.29), channel_id=1, source_target_pairs={{0,3},{1,0},{2,1},{3,2},{4,7},{5,4},{6,5},{7,6},{8,11},{9,8},{10,9... | collective-permute-start | bytes 3145736 | tf_op jit(solution)/shard_map/ppermute | solution.py:97
  112.8 1.0 fusion.41
  113.9 0.1 collective-permute-start.11
  114.0 1.5 collective-permute-start.10
  115.5 1.0 convolution_add_fusion.5
  116.6 1.0 fusion.4
  117.6 0.2 constant_dynamic-update-slice_fusion.10
  117.8 19.1 %collective-permute-done.9 = f32[4,256,256]{1,2,0:T(8,128)S(1)} collective-permute-done((f32[4,256,256]{1,2,0:T(8,128)S(1)}, f32[4,256,256]{1,2,0:T(8,128)S(1)}, u32[]{:S(2)}, u32[]{:S(2)}) %collective-permute-start.9) | collective-permute-done | bytes 1048608 | tf_op jit(solution)/shard_map/ppermute | solution.py:97
  137.0 24.3 %collective-permute-done.10 = f32[4,256,256]{1,2,0:T(8,128)S(1)} collective-permute-done((f32[4,256,256]{1,2,0:T(8,128)S(1)}, f32[4,256,256]{1,2,0:T(8,128)S(1)}, u32[]{:S(2)}, u32[]{:S(2)}) %collective-permute-start.10) | collective-permute-done | bytes 1048608 | tf_op jit(solution)/shard_map/ppermute | solution.py:97
  161.4 0.1 constant_dynamic-update-slice_fusion.7
  161.5 0.1 constant_dynamic-update-slice_fusion.6
  161.7 0.1 constant_dynamic-update-slice_fusion.3
  161.8 2.4 %constant_dynamic-slice_fusion = f32[4,256,1024]{1,2,0:T(8,128)} fusion(f32[4,256,2048]{1,2,0:T(8,128)S(1)} %constant_dynamic-update-slice_fusion.3, s32[]{:T(128)S(6)} %select_n.69), kind=kLoop, calls=%fused_computation.123 | loop fusion | bytes 8388612 | tf_op jit(solution)/shard_map/dynamic_slice | solution.py:13
  164.1 5.3 %copy.32 = f32[4,256,1024]{2,1,0:T(8,128)} copy(f32[4,256,1024]{1,2,0:T(8,128)} %constant_dynamic-slice_fusion) | data formatting | bytes 8388608 | tf_op jit(solution)/shard_map/dynamic_slice | solution.py:13
  (57 shorter events, 0.6 us)
Async XLA Ops:
  0.0 14.4 %copy-start = (f32[256]{0:T(256)S(1)}, f32[256]{0:T(256)}, u32[]{:S(2)}) copy-start(f32[256]{0:T(256)} %param.12) | copy-start | bytes 3076
  0.0 8.8 %copy-start.5 = (s32[256]{0:T(256)S(1)}, s32[256]{0:T(256)}, u32[]{:S(2)}) copy-start(s32[256]{0:T(256)} %param.10) | copy-start | bytes 3076
  0.0 8.8 %copy-start.4 = (f32[256,1024]{1,0:T(8,128)S(1)}, f32[256,1024]{1,0:T(8,128)}, u32[]{:S(2)}) copy-start(f32[256,1024]{1,0:T(8,128)} %param.9) | copy-start | bytes 3145732
  3.7 5.3 %copy-start.2 = (f32[1024]{0:T(1024)S(1)}, f32[1024]{0:T(1024)}, u32[]{:S(2)}) copy-start(f32[1024]{0:T(1024)} %param.13) | copy-start | bytes 12292
  3.7 52.9 %collective-permute-start.8 = (f32[4,256,256]{2,1,0:T(8,128)}, f32[4,256,256]{2,1,0:T(8,128)S(1)}, u32[]{:S(2)}, u32[]{:S(2)}) collective-permute-start(f32[4,256,256]{2,1,0:T(8,128)} %get-tuple-element.24), channel_id=1, source_target_pairs={{0,3},{1,0},{2,1},{3,2},{4,7},{5,4},{6,5},{7,6},{8,11},{9,8},{10,9... | collective-permute-start | bytes 3145736 | tf_op jit(solution)/shard_map/ppermute | solution.py:54
  7.7 46.3 %collective-permute-start.6 = (f32[4,256,256]{2,1,0:T(8,128)}, f32[4,256,256]{2,1,0:T(8,128)}, u32[]{:S(2)}, u32[]{:S(2)}) collective-permute-start(f32[4,256,256]{2,1,0:T(8,128)} %get-tuple-element.25), channel_id=1, source_target_pairs={{0,1},{1,2},{2,3},{3,0},{4,5},{5,6},{6,7},{7,4},{8,9},{9,10},{10,1... | collective-permute-start | bytes 3145736 | tf_op jit(solution)/shard_map/ppermute | solution.py:54
  7.7 47.6 %collective-permute-start.7 = (f32[4,256,256]{2,1,0:T(8,128)}, f32[4,256,256]{2,1,0:T(8,128)}, u32[]{:S(2)}, u32[]{:S(2)}) collective-permute-start(f32[4,256,256]{2,1,0:T(8,128)} %get-tuple-element.26), channel_id=1, source_target_pairs={{0,2},{1,3},{2,0},{3,1},{4,6},{5,7},{6,4},{7,5},{8,10},{9,11},{10,... | collective-permute-start | bytes 3145736 | tf_op jit(solution)/shard_map/ppermute | solution.py:54
  8.9 5.4 %copy-start.6 = (s32[4,2]{0,1:T(2,128)S(1)}, s32[4,2]{0,1:T(2,128)}, u32[]{:S(2)}) copy-start(s32[4,2]{0,1:T(2,128)} %param.11) | copy-start | bytes 100
  11.9 44.8 %collective-permute-start.3 = (f32[264,1024]{1,0:T(8,128)}, f32[264,1024]{1,0:T(8,128)}, u32[]{:S(2)}, u32[]{:S(2)}) collective-permute-start(f32[264,1024]{1,0:T(8,128)} %pad_maximum_fusion), channel_id=1, source_target_pairs={{24,0},{0,8},{8,16},{16,24},{12,4},{20,12},{28,20},{4,28},{25,1},{... | collective-permute-start | bytes 3244040 | tf_op jit(solution)/shard_map/ppermute | solution.py:22
  13.5 47.7 %collective-permute-start.1 = (f32[264,1024]{1,0:T(8,128)}, f32[264,1024]{1,0:T(8,128)}, u32[]{:S(2)}, u32[]{:S(2)}) collective-permute-start(f32[264,1024]{1,0:T(8,128)} %pad_maximum_fusion), channel_id=1, source_target_pairs={{28,0},{4,8},{12,16},{20,24},{8,4},{16,12},{24,20},{0,28},{29,1},{... | collective-permute-start | bytes 3244040 | tf_op jit(solution)/shard_map/ppermute | solution.py:22
  54.0 38.6 %collective-permute-start = (f32[264,1024]{1,0:T(8,128)}, f32[264,1024]{1,0:T(8,128)S(1)}, u32[]{:S(2)}, u32[]{:S(2)}) collective-permute-start(f32[264,1024]{1,0:T(8,128)} %pad_maximum_fusion), channel_id=1, source_target_pairs={{0,4},{8,12},{16,20},{24,28},{4,0},{12,8},{20,16},{28,24},{1,5},{9... | collective-permute-start | bytes 3244040 | tf_op jit(solution)/shard_map/ppermute | solution.py:22
  65.1 30.7 %collective-permute-start.4 = (f32[264,1024]{1,0:T(8,128)}, f32[264,1024]{1,0:T(8,128)S(1)}, u32[]{:S(2)}, u32[]{:S(2)}) collective-permute-start(f32[264,1024]{1,0:T(8,128)} %collective-permute-done.3), channel_id=1, source_target_pairs={{4,0},{12,8},{20,16},{28,24},{5,1},{13,9},{21,17},{29,25},{6,2},{1... | collective-permute-start | bytes 3244040 | tf_op jit(solution)/shard_map/ppermute | solution.py:22
  66.4 29.4 %collective-permute-start.5 = (f32[264,1024]{1,0:T(8,128)}, f32[264,1024]{1,0:T(8,128)S(1)}, u32[]{:S(2)}, u32[]{:S(2)}) collective-permute-start(f32[264,1024]{1,0:T(8,128)} %collective-permute-done.1), channel_id=1, source_target_pairs={{12,4},{20,12},{28,20},{4,28},{13,5},{21,13},{29,21},{5,29},{14,6}... | collective-permute-start | bytes 3244040 | tf_op jit(solution)/shard_map/ppermute | solution.py:22
  67.3 28.9 %collective-permute-start.2 = (f32[264,1024]{1,0:T(8,128)}, f32[264,1024]{1,0:T(8,128)S(1)}, u32[]{:S(2)}, u32[]{:S(2)}) collective-permute-start(f32[264,1024]{1,0:T(8,128)} %collective-permute-done.1), channel_id=1, source_target_pairs={{0,4},{8,12},{16,20},{24,28},{4,0},{12,8},{20,16},{28,24},{1,5},{9... | collective-permute-start | bytes 3244040 | tf_op jit(solution)/shard_map/ppermute | solution.py:22
  77.3 3.0 %copy-start.3 = (f32[4,256,1024]{2,1,0:T(8,128)S(1)}, f32[4,256,1024]{2,1,0:T(8,128)}, u32[]{:S(2)}) copy-start(f32[4,256,1024]{2,1,0:T(8,128)} %param.8) | copy-start | bytes 12582916
  110.4 26.5 %collective-permute-start.9 = (f32[4,256,256]{1,2,0:T(8,128)S(1)}, f32[4,256,256]{1,2,0:T(8,128)S(1)}, u32[]{:S(2)}, u32[]{:S(2)}) collective-permute-start(f32[4,256,256]{1,2,0:T(8,128)S(1)} %get-tuple-element.29), channel_id=1, source_target_pairs={{0,3},{1,0},{2,1},{3,2},{4,7},{5,4},{6,5},{7,6},{8,11},{9,8},{10,9... | collective-permute-start | bytes 3145736 | tf_op jit(solution)/shard_map/ppermute | solution.py:97
  113.9 47.5 %collective-permute-start.11 = (f32[4,256,256]{1,2,0:T(8,128)S(1)}, f32[4,256,256]{1,2,0:T(8,128)S(1)}, u32[]{:S(2)}, u32[]{:S(2)}) collective-permute-start(f32[4,256,256]{1,2,0:T(8,128)S(1)} %get-tuple-element.27), channel_id=1, source_target_pairs={{0,1},{1,2},{2,3},{3,0},{4,5},{5,6},{6,7},{7,4},{8,9},{9,10},{10,1... | collective-permute-start | bytes 3145736 | tf_op jit(solution)/shard_map/ppermute | solution.py:97
  114.0 47.3 %collective-permute-start.10 = (f32[4,256,256]{1,2,0:T(8,128)S(1)}, f32[4,256,256]{1,2,0:T(8,128)S(1)}, u32[]{:S(2)}, u32[]{:S(2)}) collective-permute-start(f32[4,256,256]{1,2,0:T(8,128)S(1)} %get-tuple-element.28), channel_id=1, source_target_pairs={{0,2},{1,3},{2,0},{3,1},{4,6},{5,7},{6,4},{7,5},{8,10},{9,11},{10,... | collective-permute-start | bytes 3145736 | tf_op jit(solution)/shard_map/ppermute | solution.py:97
  161.8 7.7 %copy-start.1 = (f32[256]{0:T(256)S(1)}, f32[256]{0:T(256)}, u32[]{:S(2)}) copy-start(f32[256]{0:T(256)} %param.12) | copy-start | bytes 3076
